TPU v7x, 512 devices: a whole 4x8x8 slice. The times are simulated.
512 devices in a mesh: req: 128 (over y, z, core), mlp: 4 (over x).
Axes of the slice: x: 4, y: 8, z: 8, core: 2. Of those that a mesh axis runs over, the one named last changes fastest.
Arguments:
- residual: bfloat16 [32768, 2048], P('req'), may hold values from -20 to 20
- query_rows: bfloat16 [32768, 2048], P('req', 'mlp'), may hold values from -6 to 6
- value_rows: bfloat16 [32768, 2048], P('req', 'mlp'), may hold values from -6 to 6
- forget_logit: float32 [32768, 2048], P('req', 'mlp'), may hold values from 0 to 40
- slot_kind: int32 [32768], P('req'), may hold values from 0 to 2, as said below
- head_gain: float32 [2048], P('mlp'), may hold values from 0.1 to 1.9
- out_weight: bfloat16 [2048, 2048], P('mlp', 'req'), may hold values from -0.125 to 0.125
- ffn_gain: float32 [2048], replicated, may hold values from 0.1 to 1.9
- gate_weight: bfloat16 [2048, 3072], P('req', 'mlp'), may hold values from -0.125 to 0.125
- up_weight: bfloat16 [2048, 3072], P('req', 'mlp'), may hold values from -0.125 to 0.125
- down_weight: bfloat16 [3072, 2048], P('mlp', 'req'), may hold values from -0.109375 to 0.109375
Outputs:
- layer_out: bfloat16 [32768, 2048], P('req', 'mlp')
Inputs may be any that keep to these rules, and one draw needn't show every extreme that they name: `slot_kind`: slots 0 to 24575 hold one prompt: slot 0 has kind 2, the others kind 1. Every other block of 256 slots holds short requests packed from its first slot, then empty slots; a short request has at most 32 tokens, the first request of each such block exactly 32. Over all 32768 slots exactly 26624 are live.
All inputs are finite; a program needn't handle non-finite values.
Results may differ from a plain program's by a relative error of at most 0.0163.
Values may be sent and summed in bfloat16 or wider, within the bound.
No kernel may reach another device: no remote copies, remote signals or barrier semaphores. Data moves between devices by JAX's collectives and lax.ppermute only.
A program may use at most 128 MiB of HBM per device.

v0:
```python
import jax
import jax.numpy as jnp
from jax import lax
from jax.sharding import PartitionSpec as P

HEAD = 128
SPAN = 32


def carried_in(part, axis, combine, identity):
    place = lax.axis_index(axis)
    gathered = jax.tree.map(lambda a: lax.all_gather(a, axis), part)
    state = jax.tree.map(lambda a, e: jnp.zeros_like(a) + jnp.asarray(e, a.dtype), part, identity)

    def one(hop, state):
        return combine(
            state, jax.tree.map(lambda a: lax.dynamic_index_in_dim(a, hop, 0, False), gathered)
        )

    return lax.fori_loop(0, place, one, state)


def span_step(passed_state, pieces):
    query_block, key_block, value_block, g_block = pieces
    top_precision = lax.Precision.HIGHEST
    inside_block_term = jnp.cumsum(g_block, axis=0)
    between_blocks_term = jnp.einsum(
        "owu,wuj->owj",
        query_block * jnp.exp(inside_block_term),
        passed_state,
        precision=top_precision,
    )
    length = g_block.shape[0]
    causal = jnp.arange(length)[:, None] >= jnp.arange(length)[None, :]
    causal = causal[:, :, None, None]
    gap_log = jnp.where(causal, inside_block_term[:, None] - inside_block_term[None, :], 0.0)
    decay_pairs = jnp.where(causal, jnp.exp(gap_log), 0.0)
    scores = jnp.einsum(
        "tnk,tsnk->tsn", query_block, decay_pairs * key_block[None], precision=top_precision
    )
    intra_part = jnp.einsum("tsn,snv->tnv", scores, value_block, precision=top_precision)
    final_decay_sum = inside_block_term[-1]
    updated_state = jnp.exp(final_decay_sum)[:, :, None] * passed_state + jnp.einsum(
        "weq,wel->eql",
        key_block * jnp.exp(final_decay_sum[None] - inside_block_term),
        value_block,
        precision=top_precision,
    )
    return (updated_state, between_blocks_term + intra_part)


def compose(earlier, later):
    return (
        earlier[0] * later[0],
        later[0][:, :, None] * earlier[1] + later[1],
        earlier[2] + later[2],
    )


def on_device(
    residual,
    query_rows,
    value_rows,
    forget_logit,
    slot_kind,
    head_gain,
    out_weight,
    ffn_gain,
    gate_weight,
    up_weight,
    down_weight,
):
    slot_total = residual.shape[0]
    quarter = query_rows.shape[1]
    heads_here = quarter // HEAD
    live_mask = slot_kind > 0
    first_mask = slot_kind == 2
    log_forget = jnp.where(
        first_mask[:, None],
        -80.0,
        jnp.where(live_mask[:, None], -jax.nn.softplus(-forget_logit), 0.0),
    )
    key_gate = jnp.where(live_mask[:, None], jax.nn.sigmoid(-forget_logit), 0.0)
    shape4 = (slot_total // SPAN, SPAN, heads_here, HEAD)
    q_all = query_rows.astype(jnp.float32).reshape(shape4)
    v_all = value_rows.astype(jnp.float32).reshape(shape4)
    k_all = key_gate.reshape(shape4)
    g_all = log_forget.reshape(shape4)
    zero_state = jnp.zeros((heads_here, HEAD, HEAD), jnp.float32)
    decay_whole = jnp.exp(jnp.sum(log_forget, axis=0)).reshape(heads_here, HEAD)
    live_count = jnp.sum(live_mask.astype(jnp.float32))
    neutral = (jnp.ones_like(decay_whole), jnp.zeros_like(zero_state), jnp.zeros((), jnp.float32))
    end_state, local_out = lax.scan(span_step, zero_state, (q_all, k_all, v_all, g_all))
    leading_decay = carried_in((decay_whole, end_state, live_count), "req", compose, neutral)
    within_all = jnp.cumsum(g_all, axis=1)
    block_total = within_all[:, -1]
    before_block = jnp.cumsum(block_total, axis=0) - block_total
    query_damped = q_all * jnp.exp(within_all + before_block[:, None])
    heads_out = local_out + jnp.einsum(
        "mosf,sfl->mosl", query_damped, leading_decay[1], precision=lax.Precision.HIGHEST
    )
    heads_out = heads_out.reshape(slot_total, heads_here, HEAD)
    mean_sq = jnp.mean(heads_out * heads_out, axis=-1, keepdims=True)
    head_normed = (
        heads_out / jnp.sqrt(mean_sq + 1e-06) * head_gain.reshape(heads_here, HEAD)
    ).astype(jnp.bfloat16)
    head_normed = head_normed.reshape(slot_total, quarter)
    partial_rows = jnp.dot(
        head_normed,
        lax.all_gather(out_weight, "req", axis=1, tiled=True),
        preferred_element_type=jnp.float32,
    )
    mixed_sum = lax.psum(partial_rows.astype(jnp.bfloat16), "mlp").astype(jnp.float32)
    stream = (residual.astype(jnp.float32) + mixed_sum).astype(jnp.bfloat16)
    my_cols = lax.axis_index("mlp") * quarter
    rows_f = stream.astype(jnp.float32)
    ffn_in = (
        rows_f / jnp.sqrt(jnp.mean(rows_f * rows_f, axis=-1, keepdims=True) + 1e-05) * ffn_gain
    ).astype(jnp.bfloat16)
    gate_acc = jnp.dot(
        ffn_in,
        lax.all_gather(gate_weight, "req", axis=0, tiled=True),
        preferred_element_type=jnp.float32,
    )
    up_acc = jnp.dot(
        ffn_in,
        lax.all_gather(up_weight, "req", axis=0, tiled=True),
        preferred_element_type=jnp.float32,
    )
    hidden = (jax.nn.silu(gate_acc) * up_acc).astype(jnp.bfloat16)
    terms = jnp.dot(
        hidden,
        lax.all_gather(down_weight, "req", axis=1, tiled=True),
        preferred_element_type=jnp.float32,
    )
    ffn_out = lax.psum_scatter(
        terms.astype(jnp.bfloat16), "mlp", scatter_dimension=1, tiled=True
    ).astype(jnp.float32)
    own_cols = lax.dynamic_slice_in_dim(stream, my_cols, quarter, 1).astype(jnp.float32)
    result = (own_cols + ffn_out).astype(jnp.bfloat16)
    layer_out = jnp.where(live_mask[:, None], result, jnp.zeros_like(result))
    return layer_out


def solution(mesh):
    return jax.shard_map(
        on_device,
        mesh=mesh,
        in_specs=(
            P("req", None),
            P("req", "mlp"),
            P("req", "mlp"),
            P("req", "mlp"),
            P("req"),
            P("mlp"),
            P("mlp", "req"),
            P(),
            P("req", "mlp"),
            P("req", "mlp"),
            P("mlp", "req"),
        ),
        out_specs=P("req", "mlp"),
        check_vma=False,
    )
```

profile of v0, /device:TPU:8, one launch (start us, length us, event | category | flops | bytes accessed | tf_op | source)
XLA Modules:
  0.0 706.2 jit_solution(7420464183667757412)
XLA Ops:
  9.6 50.4 %while.27 = (s32[]{:T(128)}, f32[4,128,128]{2,1,0:T(8,128)S(1)}, f32[8,32,4,128]{3,1,0,2:T(8,128)S(1)}, f32[8,32,4,128]{3,2,1,0:T(4,128)S(1)}, f32[8,32,4,128]{3...) while((s32[]{:T(128)}, f32[4,128,128]{2,1,0:T(8,128)S(1)}, ...), condition=%wide.region_2.3_spmd.clone, body=%wide.region_0.2_spmd.clone.sunk | while | flops 65848320 | bytes 6453368 | solution.py:93
  9.7 1.6 select_multiply_fusion.2
  11.3 3.3 fusion.68
  17.6 3.3 fusion.68
  23.9 3.3 fusion.68
  30.2 3.3 fusion.68
  36.5 3.3 fusion.68
  42.8 3.3 fusion.68
  49.1 3.3 fusion.68
  55.4 3.3 fusion.68
  62.4 56.7 %all_gather.23 = f32[128,4,128]{2,1,0:T(4,128)S(1)} all-gather(f32[1,4,128]{2,1,0:T(4,128)S(1)} %exponential_bitcast_fusion), channel_id=1, replica_groups=mesh['req'=128,'mlp'=4] {'req'}, dimensions={0}, use_global_device_ids=true | all-gather | bytes 264192 | tf_op jit(solution)/shard_map/all_gather | solution.py:12
  119.1 87.6 %all-gather.15.cloned.1.call-done = f32[512,128,128]{2,1,0:T(8,128)} async-done(((f32[4,128,128]{2,1,0:T(8,128)}), f32[512,128,128]{2,1,0:T(8,128)}) %all-gather.15.cloned.1.call-update) | async-done | bytes 33554448 | tf_op jit(solution)/shard_map/all_gather | solution.py:12
  206.7 18.6 %while.26 = (s32[]{:T(128)}, f32[4,128,128]{2,1,0:T(8,128)S(1)}, s32[]{:T(128)}, f32[128,4,128]{2,1,0:T(4,128)S(1)}, f32[128,4,128,128]{3,2,1,0:T(8,128)}, /*index=5*/s32[]{:T(128)}, s32[]{:T(128)}, s32[]{:T(128)}) while((s32[]{:T(128)}, f32[4,128,128]{2,1,0:T(8,128)S(1)}, s32[]{:T(128)}, f32[128,4,128]{2,1,0:T(4,128)S(1)}, ...), condition=%wide.region_5.6_spmd, body=%wide.region_4.5_spmd.sunk | while | flops 131077 | bytes 792703 | solution.py:20
  226.6 63.5 %all-gather.7.cloned.1.call-done = bf16[512,2048]{0,1:T(8,128)(2,1)} async-done(((bf16[512,16]{0,1:T(8,128)(2,1)}), bf16[512,2048]{0,1:T(8,128)(2,1)}) %all-gather.7.cloned.1.call-update) | async-done | bytes 2097168 | tf_op jit(solution)/shard_map/all_gather | solution.py:110
  290.5 3.4 convolution_convert_fusion
  295.9 114.3 %all-reduce.2.cloned.1.call-done = bf16[256,2048]{1,0:T(8,128)(2,1)} async-done(((bf16[256,2048]{1,0:T(8,128)(2,1)}), bf16[256,2048]{1,0:T(8,128)(2,1)}) %all-reduce.2.cloned.1.call-update) | async-done | bytes 1048592 | tf_op jit(solution)/shard_map/psum | solution.py:113
  410.2 1.7 fusion.18
  412.0 85.4 %all-gather.9.cloned.1.call-done = bf16[2048,768]{1,0:T(8,128)(2,1)} async-done(((bf16[16,768]{1,0:T(8,128)(2,1)}), bf16[2048,768]{1,0:T(8,128)(2,1)}) %all-gather.9.cloned.1.call-update) | async-done | bytes 3145744 | tf_op jit(solution)/shard_map/all_gather | solution.py:122
  497.4 2.9 fusion.36
  500.3 80.7 %all-gather.11.cloned.1.call-done = bf16[2048,768]{1,0:T(8,128)(2,1)} async-done(((bf16[16,768]{1,0:T(8,128)(2,1)}), bf16[2048,768]{1,0:T(8,128)(2,1)}) %all-gather.11.cloned.1.call-update) | async-done | bytes 3145744 | tf_op jit(solution)/shard_map/all_gather | solution.py:127
  581.1 83.7 %all-gather.13.cloned.1.call-done = bf16[768,2048]{0,1:T(8,128)(2,1)} async-done(((bf16[768,16]{0,1:T(8,128)(2,1)}), bf16[768,2048]{0,1:T(8,128)(2,1)}) %all-gather.13.cloned.1.call-update) | async-done | bytes 3145744 | tf_op jit(solution)/shard_map/all_gather | solution.py:133
  664.8 6.1 convolution_convert_fusion.1
  670.9 26.7 %reduce-scatter.2.cloned.1.call-done = bf16[256,512]{1,0:T(8,128)(2,1)} async-done(((bf16[256,2048]{1,0:T(8,128)(2,1)}), bf16[256,512]{1,0:T(8,128)(2,1)}) %reduce-scatter.2.cloned.1.call-update) | async-done | bytes 262160 | tf_op jit(solution)/shard_map/reduce_scatter | solution.py:136
  697.6 1.8 fusion.30
  (160 shorter events, 48.5 us)
Async XLA Ops:
  6.5 2.5 copy-start.2
  6.5 200.1 %all-gather.15.cloned.1.call-start = ((), (), s32[]{:S(2)}) async-start(), calls=%async_computation.7 | async-start | bytes 33816576 | tf_op jit(solution)/shard_map/all_gather | solution.py:12
  7.3 2.1 copy-start.3
  60.0 0.7 copy-start
  60.7 229.5 %all-gather.7.cloned.1.call-start = ((), (), s32[]{:S(2)}) async-start(), calls=%async_computation.1 | async-start | bytes 2113536 | tf_op jit(solution)/shard_map/all_gather | solution.py:110
  61.4 348.8 %all-reduce.2.cloned.1.call-start = ((), (), s32[]{:S(2)}) async-start(), calls=%async_computation.2 | async-start | bytes 2097152 | tf_op jit(solution)/shard_map/psum | solution.py:113
  225.3 65.2 %copy-start.5 = (f32[512]{0:T(512)S(1)}, f32[512]{0:T(512)}, u32[]{:S(2)}) copy-start(f32[512]{0:T(512)} %param.20) | copy-start | bytes 6148
  290.5 119.7 %copy-start.1 = (bf16[256,2048]{1,0:T(8,128)(2,1)S(1)}, bf16[256,2048]{1,0:T(8,128)(2,1)}, u32[]{:S(2)}) copy-start(bf16[256,2048]{1,0:T(8,128)(2,1)} %param.15) | copy-start | bytes 3145732
  293.9 203.5 %copy-start.4 = (f32[2048]{0:T(1024)S(1)}, f32[2048]{0:T(1024)}, u32[]{:S(2)}) copy-start(f32[2048]{0:T(1024)} %param.22) | copy-start | bytes 24580
  293.9 203.4 %all-gather.9.cloned.1.call-start = ((), (), s32[]{:S(2)}) async-start(), calls=%async_computation.3 | async-start | bytes 3170304 | tf_op jit(solution)/shard_map/all_gather | solution.py:122
  294.5 286.5 %all-gather.11.cloned.1.call-start = ((), (), s32[]{:S(2)}) async-start(), calls=%async_computation.4 | async-start | bytes 3170304 | tf_op jit(solution)/shard_map/all_gather | solution.py:127
  295.1 369.7 %all-gather.13.cloned.1.call-start = ((), (), s32[]{:S(2)}) async-start(), calls=%async_computation.5 | async-start | bytes 3170304 | tf_op jit(solution)/shard_map/all_gather | solution.py:133
  295.7 401.9 %reduce-scatter.2.cloned.1.call-start = ((), (), s32[]{:S(2)}) async-start(), calls=%async_computation.6 | async-start | bytes 1310720 | tf_op jit(solution)/shard_map/reduce_scatter | solution.py:136
Sparse Core Ops, SparseCore 0:
  60.8 145.7 all-gather.14
  209.8 80.3 all-gather.6
  294.1 116.1 all-reduce.1
  413.2 84.1 all-gather.8
  500.3 80.6 all-gather.10
  584.0 80.6 all-gather.12
  671.0 26.5 reduce-scatter.1
where the time goes:
time: 710 us; the launch traced here: 706 us
  waiting for transfers between devices  544 us (77%)
  blocking collectives  56.7 us (8%)
  matrix products  49.3 us (7%)
  other arithmetic  38 us (5%)
  between operations  13.7 us (2%)
    psum x1, waiting for transfers between devices, on_device(): lax.psum(partial_rows.astype(jnp.bfloat16), 'mlp').astype(jnp.float32)  114 us
    all_gather x1, waiting for transfers between devices, carried_in(): gathered = jax.tree.map(lambda a: lax.all_gather(a, axis), part)  87.6 us
    all_gather x1, waiting for transfers between devices, on_device(): lax.all_gather(gate_weight, 'req', axis=0, tiled=True)  85.4 us
    all_gather x1, waiting for transfers between devices, on_device(): lax.all_gather(down_weight, 'req', axis=1, tiled=True)  83.7 us
    all_gather x1, waiting for transfers between devices, on_device(): lax.all_gather(up_weight, 'req', axis=0, tiled=True)  80.7 us
    all_gather x1, waiting for transfers between devices, on_device(): lax.all_gather(out_weight, 'req', axis=1, tiled=True)  63.5 us
    all_gather x1, blocking collectives, carried_in(): gathered = jax.tree.map(lambda a: lax.all_gather(a, axis), part)  56.7 us
    dot_general x8, matrix products, span_step(): jnp.einsum('tnk,tsnk->tsn', query_block, decay_pairs * key_block[None], p...  26.8 us
  transfers between devices with their start and end apart: 7, of which 7 were waited for; matrix products, arithmetic and copies ran while one was open for 4% of the time, Pallas kernels for 0%

commit v1 on v0

--- a/solution.py
+++ b/solution.py
@@ -5,6 +5,13 @@
 
 HEAD = 128
 SPAN = 32
+
+
+def launch_tables_all(a0, axis_no):
+    u1 = jnp.stack([a0] * jax.lax.axis_size("req"))
+    big = jax.lax.all_to_all(u1, axis_name="req", concat_axis=0, split_axis=0)
+    w1 = jnp.concatenate(big, axis=axis_no)
+    return w1
 
 
 def carried_in(part, axis, combine, identity):
@@ -128,11 +135,7 @@
         preferred_element_type=jnp.float32,
     )
     hidden = (jax.nn.silu(gate_acc) * up_acc).astype(jnp.bfloat16)
-    terms = jnp.dot(
-        hidden,
-        lax.all_gather(down_weight, "req", axis=1, tiled=True),
-        preferred_element_type=jnp.float32,
-    )
+    terms = jnp.dot(hidden, launch_tables_all(down_weight, 1), preferred_element_type=jnp.float32)
     ffn_out = lax.psum_scatter(
         terms.astype(jnp.bfloat16), "mlp", scatter_dimension=1, tiled=True
     ).astype(jnp.float32)

time: 710 us -> 632 us (0.89)
  waiting for transfers between devices: 544 us -> 390 us
  starting transfers between devices: 0.42 us -> 72.4 us
    all_gather x1 -> x0, waiting for transfers between devices: 83.7 us -> none  [on_device(): lax.all_gather(down_weight, 'req', axis=1, tiled=True)]
    psum x1, waiting for transfers between devices: 114 us -> 40.7 us  [on_device(): lax.psum(partial_rows.astype(jnp.bfloat16), 'mlp').astype(jnp.float32)]
    all_to_all x0 -> x1, starting transfers between devices: none -> 72 us  [launch_tables_all(): big = jax.lax.all_to_all(u1, axis_name='req', concat_axis=0, split_axis=0)]
  transfers between devices with their start and end apart: 7 -> 7, of which waited for: 7 -> 6; matrix products, arithmetic and copies ran while one was open for 4% -> 5% of each run, Pallas kernels for 0% -> 0%
where the time goes in v1:
time: 632 us; the launch traced here: 628 us
  waiting for transfers between devices  390 us (62%)
  starting transfers between devices  72.4 us (11%)
  blocking collectives  56.7 us (9%)
  matrix products  49.9 us (8%)
  other arithmetic  39.2 us (6%)
  between operations  13.7 us (2%)
    all_gather x1, waiting for transfers between devices, on_device(): lax.all_gather(gate_weight, 'req', axis=0, tiled=True)  90.1 us
    all_gather x1, waiting for transfers between devices, carried_in(): gathered = jax.tree.map(lambda a: lax.all_gather(a, axis), part)  87.6 us
    all_gather x1, waiting for transfers between devices, on_device(): lax.all_gather(up_weight, 'req', axis=0, tiled=True)  79.6 us
    all_to_all x1, starting transfers between devices, launch_tables_all(): big = jax.lax.all_to_all(u1, axis_name='req', concat_axis=0, split_axis=0)  72 us
    all_gather x1, waiting for transfers between devices, on_device(): lax.all_gather(out_weight, 'req', axis=1, tiled=True)  63.6 us
    all_gather x1, blocking collectives, carried_in(): gathered = jax.tree.map(lambda a: lax.all_gather(a, axis), part)  56.7 us
    psum x1, waiting for transfers between devices, on_device(): lax.psum(partial_rows.astype(jnp.bfloat16), 'mlp').astype(jnp.float32)  40.7 us
    reduce_scatter x1, waiting for transfers between devices, on_device(): lax.psum_scatter(terms.astype(jnp.bfloat16), 'mlp', scatter_dimension=1,...  26.8 us
  transfers between devices with their start and end apart: 7, of which 6 were waited for; matrix products, arithmetic and copies ran while one was open for 5% of the time, Pallas kernels for 0%

profile of v1, /device:TPU:8, one launch (start us, length us, event | category | flops | bytes accessed | tf_op | source)
XLA Modules:
  0.0 627.6 jit_solution(7775289187042406453)
XLA Ops:
  9.6 50.4 %while.27 = (s32[]{:T(128)}, f32[4,128,128]{2,1,0:T(8,128)S(1)}, f32[8,32,4,128]{3,1,0,2:T(8,128)S(1)}, f32[8,32,4,128]{3,2,1,0:T(4,128)S(1)}, f32[8,32,4,128]{3...) while((s32[]{:T(128)}, f32[4,128,128]{2,1,0:T(8,128)S(1)}, ...), condition=%wide.region_2.3_spmd.clone, body=%wide.region_0.2_spmd.clone.sunk | while | flops 65848320 | bytes 6453368 | solution.py:100
  11.3 3.3 fusion.68
  17.6 3.3 fusion.68
  23.9 3.3 fusion.68
  30.2 3.3 fusion.68
  36.5 3.3 fusion.68
  42.8 3.3 fusion.68
  49.1 3.3 fusion.68
  55.4 3.3 fusion.68
  62.4 56.7 %all_gather.20 = f32[128,4,128]{2,1,0:T(4,128)S(1)} all-gather(f32[1,4,128]{2,1,0:T(4,128)S(1)} %exponential_bitcast_fusion), channel_id=1, replica_groups=mesh['req'=128,'mlp'=4] {'req'}, dimensions={0}, use_global_device_ids=true | all-gather | bytes 264192 | tf_op jit(solution)/shard_map/all_gather | solution.py:19
  119.1 87.6 %all-gather.12.cloned.1.call-done = f32[512,128,128]{2,1,0:T(8,128)} async-done(((f32[4,128,128]{2,1,0:T(8,128)}), f32[512,128,128]{2,1,0:T(8,128)}) %all-gather.12.cloned.1.call-update) | async-done | bytes 33554448 | tf_op jit(solution)/shard_map/all_gather | solution.py:19
  206.7 18.6 %while.26 = (s32[]{:T(128)}, f32[4,128,128]{2,1,0:T(8,128)S(1)}, s32[]{:T(128)}, f32[128,4,128]{2,1,0:T(4,128)S(1)}, f32[128,4,128,128]{3,2,1,0:T(8,128)}, /*index=5*/s32[]{:T(128)}, s32[]{:T(128)}, s32[]{:T(128)}) while((s32[]{:T(128)}, f32[4,128,128]{2,1,0:T(8,128)S(1)}, s32[]{:T(128)}, f32[128,4,128]{2,1,0:T(4,128)S(1)}, ...), condition=%wide.region_5.6_spmd, body=%wide.region_4.5_spmd.sunk | while | flops 131077 | bytes 792703 | solution.py:27
  226.6 63.6 %all-gather.6.cloned.1.call-done = bf16[512,2048]{0,1:T(8,128)(2,1)} async-done(((bf16[512,16]{0,1:T(8,128)(2,1)}), bf16[512,2048]{0,1:T(8,128)(2,1)}) %all-gather.6.cloned.1.call-update) | async-done | bytes 2097168 | tf_op jit(solution)/shard_map/all_gather | solution.py:117
  290.5 3.3 convolution_convert_fusion
  294.5 1.9 stack.2
  296.4 72.0 %all-to-all-start = ((bf16[128,768,16]{1,2,0:T(8,128)(2,1)}), bf16[128,768,16]{1,2,0:T(8,128)(2,1)S(1)}, u32[]{:S(2)}, u32[]{:S(2)}) async-start(bf16[128,768,16]{1,2,0:T(8,128)(2,1)} %stack.2), calls=%async_computation | async-start | bytes 6291456 | tf_op jit(solution)/shard_map/all_to_all | solution.py:12
  369.2 40.7 %all-reduce.2.cloned.1.call-done = bf16[256,2048]{1,0:T(8,128)(2,1)} async-done(((bf16[256,2048]{1,0:T(8,128)(2,1)}), bf16[256,2048]{1,0:T(8,128)(2,1)}) %all-reduce.2.cloned.1.call-update) | async-done | bytes 1048592 | tf_op jit(solution)/shard_map/psum | solution.py:120
  409.9 2.9 fusion.18
  412.8 90.1 %all-gather.8.cloned.1.call-done = bf16[2048,768]{1,0:T(8,128)(2,1)} async-done(((bf16[16,768]{1,0:T(8,128)(2,1)}), bf16[2048,768]{1,0:T(8,128)(2,1)}) %all-gather.8.cloned.1.call-update) | async-done | bytes 3145744 | tf_op jit(solution)/shard_map/all_gather | solution.py:129
  502.9 4.1 fusion.36
  507.0 79.6 %all-gather.10.cloned.1.call-done = bf16[2048,768]{1,0:T(8,128)(2,1)} async-done(((bf16[16,768]{1,0:T(8,128)(2,1)}), bf16[2048,768]{1,0:T(8,128)(2,1)}) %all-gather.10.cloned.1.call-update) | async-done | bytes 3145744 | tf_op jit(solution)/shard_map/all_gather | solution.py:134
  586.6 5.6 convolution_convert_fusion.1
  592.2 26.8 %reduce-scatter.2.cloned.1.call-done = bf16[256,512]{1,0:T(8,128)(2,1)} async-done(((bf16[256,2048]{1,0:T(8,128)(2,1)}), bf16[256,512]{1,0:T(8,128)(2,1)}) %reduce-scatter.2.cloned.1.call-update) | async-done | bytes 262160 | tf_op jit(solution)/shard_map/reduce_scatter | solution.py:139
  618.9 1.8 fusion.30
  (160 shorter events, 49.4 us)
Async XLA Ops:
  6.5 2.5 copy-start.1
  6.5 200.1 %all-gather.12.cloned.1.call-start = ((), (), s32[]{:S(2)}) async-start(), calls=%async_computation.7 | async-start | bytes 33816576 | tf_op jit(solution)/shard_map/all_gather | solution.py:19
  7.3 2.1 copy-start.2
  60.0 0.7 copy-start
  60.7 229.5 %all-gather.6.cloned.1.call-start = ((), (), s32[]{:S(2)}) async-start(), calls=%async_computation.2 | async-start | bytes 2113536 | tf_op jit(solution)/shard_map/all_gather | solution.py:117
  61.4 348.5 %all-reduce.2.cloned.1.call-start = ((), (), s32[]{:S(2)}) async-start(), calls=%async_computation.3 | async-start | bytes 2097152 | tf_op jit(solution)/shard_map/psum | solution.py:120
  225.3 65.2 %copy-start.5 = (f32[512]{0:T(512)S(1)}, f32[512]{0:T(512)}, u32[]{:S(2)}) copy-start(f32[512]{0:T(512)} %param.20) | copy-start | bytes 6148
  290.5 3.9 copy-start.3
  293.9 209.0 %all-gather.8.cloned.1.call-start = ((), (), s32[]{:S(2)}) async-start(), calls=%async_computation.4 | async-start | bytes 3170304 | tf_op jit(solution)/shard_map/all_gather | solution.py:129
  296.4 210.6 %all-to-all-start = ((bf16[128,768,16]{1,2,0:T(8,128)(2,1)}), bf16[128,768,16]{1,2,0:T(8,128)(2,1)S(1)}, u32[]{:S(2)}, u32[]{:S(2)}) async-start(bf16[128,768,16]{1,2,0:T(8,128)(2,1)} %stack.2), calls=%async_computation | async-start | bytes 6291456 | tf_op jit(solution)/shard_map/all_to_all | solution.py:12
  368.3 134.5 %copy-start.4 = (f32[2048]{0:T(1024)S(1)}, f32[2048]{0:T(1024)}, u32[]{:S(2)}) copy-start(f32[2048]{0:T(1024)} %param.22) | copy-start | bytes 24580
  368.4 218.2 %all-gather.10.cloned.1.call-start = ((), (), s32[]{:S(2)}) async-start(), calls=%async_computation.5 | async-start | bytes 3170304 | tf_op jit(solution)/shard_map/all_gather | solution.py:134
  368.9 250.0 %reduce-scatter.2.cloned.1.call-start = ((), (), s32[]{:S(2)}) async-start(), calls=%async_computation.6 | async-start | bytes 1310720 | tf_op jit(solution)/shard_map/reduce_scatter | solution.py:139
Sparse Core Ops, SparseCore 0:
  60.8 145.7 all-gather.11
  209.8 80.3 all-gather.5
  294.0 115.8 all-reduce.1
  412.9 89.9 all-gather.7
  505.8 80.6 all-gather.9
  592.3 26.6 reduce-scatter.1
